TPU v7x, 32 devices: a whole 2x2x4 slice. The times are simulated.
32 devices in a mesh: req: 8 (over z, y), ep: 4 (over x, core).
Axes of the slice: x: 2, y: 2, z: 4, core: 2. Of those that a mesh axis runs over, the one named last changes fastest.
Arguments:
- tokens: bfloat16 [4096, 1536], P(('req', 'ep')), may hold values from -6 to 6
- seg_ids: int32 [4096], P(('req', 'ep')), may hold values from 0 to 3, never falling along the last dimension, each value on 1 to 2048 neighbouring positions
- routes: int32 [4096, 8], P(('req', 'ep')), may hold values from 0 to 39, all different within a row; in each aligned block of 128 rows (0 to 127, 128 to 255, ...) at most 48 rows name the same one
- route_weights: float32 [4096, 8], P(('req', 'ep')), may hold values from 0.05 to 0.3
- norm1_gain: float32 [1536], replicated, may hold values from 0.5 to 1.5
- norm2_gain: float32 [1536], replicated, may hold values from 0.5 to 1.5
- w_query: bfloat16 [1536, 1536], P(None, 'ep')
- key_weight: bfloat16 [1536, 512], P(None, 'ep')
- value_weight: bfloat16 [1536, 512], P(None, 'ep'), may hold values from -0.15625 to 0.15625
- w_out_attn: bfloat16 [1536, 1536], P('ep'), may hold values from -0.15625 to 0.15625
- w_in: bfloat16 [40, 1536, 1024], P('ep'), may hold values from -0.15625 to 0.15625
- w_out: bfloat16 [40, 512, 1536], P('ep'), may hold values from -0.25 to 0.25
- paged_key_value_cache: bfloat16 [96, 8, 2, 64, 64], P('req', 'ep'), may hold values from -6 to 6
- page_table: int32 [64], replicated, may hold values from 0 to 95, as said below
Outputs:
- attn_out: bfloat16 [4096, 1536], P(('req', 'ep'))
- moe_out: bfloat16 [4096, 1536], P(('req', 'ep'))
- new_cache: bfloat16 [96, 8, 2, 64, 64], P('req', 'ep')
Inputs may be any that keep to these rules, and one draw needn't show every extreme that they name: `seg_ids`: segment ids never fall along the stream; the longest prompt holds exactly half of the 4096 tokens. `routes`: each token names 8 different experts; within the rows of one device no expert is named more than 48 times, a bound that some block reaches. `page_table`: entries are distinct.
All inputs are finite; a program needn't handle non-finite values.
Results may differ from a plain program's by a relative error of at most 0.017.
Values may be sent and summed in bfloat16 or wider, within the bound.
No kernel may reach another device: no remote copies, remote signals or barrier semaphores. Data moves between devices by JAX's collectives and lax.ppermute only.
A program may use at most 192 MiB of HBM per device.

v0:
```python
import jax
import jax.numpy as jnp
from jax import lax
from jax.sharding import PartitionSpec as P

HEAD_SIZE = 64
E = 40
PAGE_TOKENS = 64
CAP = 48
norm_eps = 1e-06
score_scale = 0.015625
residual_scale = 0.22
rope_base = 10000.0
neg_fill = -1e30


def rms_scale(rows, gain):
    mean_sq = jnp.mean(rows * rows, axis=-1, keepdims=True)
    return rows * lax.rsqrt(mean_sq + norm_eps) * gain


def positions_of(segments):
    tok_index = jnp.arange(segments.shape[0], dtype=jnp.int32)
    previous = jnp.concatenate([jnp.full((1,), -1, jnp.int32), segments[:-1]])
    starts = jnp.where(segments != previous, tok_index, 0)
    return tok_index - lax.cummax(starts, axis=0)


def rotary_apply(heads_in, token_positions):
    half_dim = heads_in.shape[-1] // 2
    inverse_freq = rope_base ** (
        -jnp.arange(half_dim, dtype=jnp.float32) * 2.0 / heads_in.shape[-1]
    )
    angles = token_positions.astype(jnp.float32)[:, None] * inverse_freq[None, :]
    cos_part = jnp.cos(angles)[:, None, :]
    sine_part = jnp.sin(angles)[:, None, :]
    first_half = heads_in[..., :half_dim]
    second_half = heads_in[..., half_dim:]
    return jnp.concatenate(
        [
            first_half * cos_part - second_half * sine_part,
            second_half * cos_part + first_half * sine_part,
        ],
        axis=-1,
    )


def body(
    tokens,
    seg_ids,
    routes,
    route_weights,
    norm1_gain,
    norm2_gain,
    w_query,
    key_weight,
    value_weight,
    w_out_attn,
    w_in,
    w_out,
    paged_key_value_cache,
    page_table,
):
    tok_dev = tokens.shape[0]
    ep_count = lax.axis_size("ep")
    group_len = tok_dev * ep_count
    req_pos = lax.axis_index("req")
    all_segs = lax.all_gather(seg_ids, ("req", "ep"), axis=0, tiled=True)
    all_pos = positions_of(all_segs)
    group_start = req_pos * group_len
    group_pos = lax.dynamic_slice_in_dim(all_pos, group_start, group_len)
    group_seg = lax.dynamic_slice_in_dim(all_segs, group_start, group_len)
    normed = rms_scale(tokens.astype(jnp.float32), norm1_gain).astype(jnp.bfloat16)
    joined = jnp.concatenate([w_query, key_weight, value_weight], axis=1)
    projected = jnp.dot(
        lax.all_gather(normed, "ep", axis=0, tiled=True), joined, preferred_element_type=jnp.float32
    )
    query_width = w_query.shape[1]
    kv_width = key_weight.shape[1]
    q_heads = query_width // HEAD_SIZE
    kv_heads = kv_width // HEAD_SIZE
    heads_ratio = q_heads // kv_heads
    query_rows = rotary_apply(
        projected[:, :query_width].reshape(group_len, q_heads, HEAD_SIZE), group_pos
    ).astype(jnp.bfloat16)
    key_matrix = (
        rotary_apply(
            projected[:, query_width : query_width + kv_width].reshape(
                group_len, kv_heads, HEAD_SIZE
            ),
            group_pos,
        )
        .astype(jnp.bfloat16)
        .reshape(group_len, kv_width)
    )
    value_rows = projected[:, query_width + kv_width :].astype(jnp.bfloat16)
    query_grouped = query_rows.reshape(group_len, kv_heads, heads_ratio, HEAD_SIZE).transpose(
        1, 2, 0, 3
    )
    pages_here = paged_key_value_cache.shape[0]
    page_first = req_pos * pages_here
    q_last = group_start + group_len - 1
    seg_low = group_seg[0]
    q_index = group_start + jnp.arange(group_len, dtype=jnp.int32)
    page_cells = kv_heads * 2 * PAGE_TOKENS * HEAD_SIZE
    cache_shape = paged_key_value_cache.shape
    local_pages = page_first + jnp.arange(pages_here, dtype=jnp.int32)
    begin_at = jnp.int32(0)
    run_max = jnp.full((kv_heads, heads_ratio, group_len), neg_fill, jnp.float32)
    run_sum = jnp.zeros((kv_heads, heads_ratio, group_len), jnp.float32)
    run_acc = jnp.zeros((kv_heads, heads_ratio, group_len, HEAD_SIZE), jnp.float32)
    cache_rows = paged_key_value_cache.reshape(pages_here, page_cells)
    key_piece = lax.all_gather(key_matrix, "req", axis=0, tiled=True)
    value_piece = lax.all_gather(value_rows, "req", axis=0, tiled=True)
    n_rows = key_piece.shape[0]
    piece_pages = n_rows // PAGE_TOKENS
    keys_paged = key_piece.reshape(piece_pages, PAGE_TOKENS, kv_heads, HEAD_SIZE).transpose(
        0, 2, 1, 3
    )
    values_paged = value_piece.reshape(piece_pages, PAGE_TOKENS, kv_heads, HEAD_SIZE).transpose(
        0, 2, 1, 3
    )
    fresh = jnp.stack([keys_paged, values_paged], axis=2).reshape(piece_pages, page_cells)
    match = local_pages[:, None] == page_table[None, :]
    placed = jnp.dot(match.astype(jnp.bfloat16), fresh, preferred_element_type=jnp.float32).astype(
        jnp.bfloat16
    )
    hit = jnp.any(match, axis=1)
    cache_rows = jnp.where(hit[:, None], placed, cache_rows)
    last_seg = lax.dynamic_index_in_dim(all_segs, begin_at + n_rows - 1, keepdims=False)
    needed = (begin_at <= q_last) & (last_seg >= seg_low)
    step_rows = min(n_rows, 1024)
    turns = n_rows // step_rows

    def attend(state_in):

        def one_block(turn_idx, state_now):
            block_max, block_sum, block_acc = state_now
            row_at = turn_idx * step_rows
            key_block = lax.dynamic_slice_in_dim(key_piece, row_at, step_rows).reshape(
                step_rows, kv_heads, HEAD_SIZE
            )
            value_block = lax.dynamic_slice_in_dim(value_piece, row_at, step_rows).reshape(
                step_rows, kv_heads, HEAD_SIZE
            )
            key_index = row_at + jnp.arange(step_rows, dtype=jnp.int32)
            key_segs = lax.dynamic_slice_in_dim(all_segs, row_at, step_rows)
            allowed = (group_seg[:, None] == key_segs[None, :]) & (
                key_index[None, :] <= q_index[:, None]
            )
            scores = (
                jnp.einsum(
                    "grqd,kgd->grqk", query_grouped, key_block, preferred_element_type=jnp.float32
                )
                * score_scale
            )
            masked = jnp.where(allowed, scores, neg_fill)
            new_max = jnp.maximum(block_max, jnp.max(masked, axis=-1))
            exponent = jnp.where(allowed, jnp.exp(masked - new_max[..., None]), 0.0)
            rescale = jnp.exp(block_max - new_max)
            new_sum = block_sum * rescale + jnp.sum(exponent, axis=-1)
            new_acc = block_acc * rescale[..., None] + jnp.einsum(
                "grqk,kgd->grqd",
                exponent.astype(jnp.bfloat16),
                value_block,
                preferred_element_type=jnp.float32,
            )
            return (new_max, new_sum, new_acc)

        return lax.fori_loop(0, turns, one_block, state_in)

    run_max, run_sum, run_acc = lax.cond(
        needed, attend, lambda state_in: state_in, (run_max, run_sum, run_acc)
    )
    run_max, run_sum, run_acc, cache_flat = (run_max, run_sum, run_acc, cache_rows)
    new_cache = cache_flat.reshape(cache_shape)
    head_out = (run_acc / run_sum[..., None]).astype(jnp.bfloat16)
    head_out = head_out.transpose(2, 0, 1, 3).reshape(group_len, query_width)
    attention = lax.psum_scatter(
        jnp.dot(head_out, w_out_attn, preferred_element_type=jnp.float32).astype(jnp.bfloat16),
        "ep",
        scatter_dimension=0,
        tiled=True,
    ).astype(jnp.float32)
    attn_out = attention.astype(jnp.bfloat16)
    moe_in = rms_scale(tokens.astype(jnp.float32) + residual_scale * attention, norm2_gain).astype(
        jnp.bfloat16
    )
    ffe_width = w_out.shape[1]
    exp_here = w_in.shape[0]
    expert_ids = jnp.arange(E, dtype=jnp.int32)
    shares = jnp.sum(
        jnp.where(routes[:, :, None] == expert_ids[None, None, :], route_weights[:, :, None], 0.0),
        axis=1,
    )
    rows_all = lax.all_gather(moe_in, "ep", axis=0, tiled=True)
    shares_all = lax.all_gather(shares, "ep", axis=0, tiled=True)
    first_expert = lax.axis_index("ep") * exp_here
    shares_here = lax.dynamic_slice_in_dim(shares_all, first_expert, exp_here, 1)
    total_rows = rows_all.shape[0]
    chosen = (shares_here > 0.0).astype(jnp.int32).reshape(ep_count, tok_dev, exp_here)
    slot_in = jnp.cumsum(chosen, axis=1) - 1
    source_ids = jnp.arange(ep_count, dtype=jnp.int32)[:, None, None]
    local_slot = (source_ids * CAP + slot_in).reshape(total_rows, exp_here)
    live = (chosen > 0).reshape(total_rows, exp_here)
    slot_ids = jnp.arange(ep_count * CAP, dtype=jnp.int32)
    dispatch = (local_slot.T[:, None, :] == slot_ids[None, :, None]) & live.T[:, None, :]
    arrived = jnp.einsum(
        "esr,rd->esd", dispatch.astype(jnp.bfloat16), rows_all, preferred_element_type=jnp.float32
    ).astype(jnp.bfloat16)
    gate_up = jnp.einsum("esd,edf->esf", arrived, w_in, preferred_element_type=jnp.float32)
    activated = (jax.nn.silu(gate_up[..., :ffe_width]) * gate_up[..., ffe_width:]).astype(
        jnp.bfloat16
    )
    result = jnp.einsum(
        "esf,efd->esd", activated, w_out, preferred_element_type=jnp.float32
    ).astype(jnp.bfloat16)
    slot_weight = jnp.sum(jnp.where(dispatch, shares_here.T[:, None, :], 0.0), axis=2)
    weighted = result.astype(jnp.float32) * slot_weight[..., None]
    partial_rows = jnp.einsum(
        "esr,esd->rd",
        dispatch.astype(jnp.float32),
        weighted,
        precision=lax.Precision.HIGHEST,
        preferred_element_type=jnp.float32,
    )
    moe_out = lax.psum_scatter(
        partial_rows.astype(jnp.bfloat16), "ep", scatter_dimension=0, tiled=True
    )
    return (attn_out, moe_out, new_cache)


def solution(mesh):
    in_specs = (
        P(("req", "ep"), None),
        P(("req", "ep")),
        P(("req", "ep"), None),
        P(("req", "ep"), None),
        P(),
        P(),
        P(None, "ep"),
        P(None, "ep"),
        P(None, "ep"),
        P("ep", None),
        P("ep", None, None),
        P("ep", None, None),
        P("req", "ep", None, None, None),
        P(),
    )
    out_specs = (P(("req", "ep"), None), P(("req", "ep"), None), P("req", "ep", None, None, None))
    return jax.shard_map(body, mesh=mesh, in_specs=in_specs, out_specs=out_specs, check_vma=False)
```

profile of v0, /device:TPU:0, one launch (start us, length us, event | category | flops | bytes accessed | tf_op | source)
XLA Modules:
  0.0 372.4 jit_solution(15703386580134532242)
XLA Ops:
  7.2 1.2 fusion.57
  8.5 1.9 fusion.59
  10.5 43.2 %all-gather = s32[32,1,128]{2,1,0:T(1,128)S(1)} all-gather(s32[1,1,128]{2,1,0:T(1,128)} %bitcast.115), channel_id=1, replica_groups=mesh['req'=8,'ep'=4] {'req','ep'}, dimensions={0}, use_global_device_ids=true | all-gather | bytes 16896 | tf_op jit(solution)/shard_map/all_gather | solution.py:68
  54.5 0.3 multiply_cosine_fusion
  54.8 3.4 fusion.42
  58.4 0.9 pad_maximum_fusion.1
  59.4 0.7 slice.83
  60.2 0.6 dynamic_slice.41
  60.8 0.6 slice.42
  62.6 1.2 slice.61
  64.3 30.8 %all-gather.8.cloned.1.call-done = bf16[4096,128]{0,1:T(8,128)(2,1)} async-done(((bf16[512,128]{0,1:T(8,128)(2,1)}), bf16[4096,128]{0,1:T(8,128)(2,1)}) %all-gather.8.cloned.1.call-update) | async-done | bytes 1048592 | tf_op jit(solution)/shard_map/all_gather | solution.py:113
  95.1 41.8 %all-gather.10.cloned.1.call-done = bf16[4096,128]{1,0:T(8,128)(2,1)} async-done(((bf16[512,128]{1,0:T(8,128)(2,1)}), bf16[4096,128]{1,0:T(8,128)(2,1)}) %all-gather.10.cloned.1.call-update) | async-done | bytes 1048592 | tf_op jit(solution)/shard_map/all_gather | solution.py:114
  136.9 99.9 %conditional.1 = (f32[2,3,512]{2,1,0:T(4,128)}, f32[2,3,512,64]{2,3,1,0:T(8,128)}) conditional(s32[]{:T(128)} %convert_element_type.66, () %tuple.30, (s32[]{:T(128)}, s32[512]{0:T(512)S(1)}, s32[512]{0:T(512)S(1)}, s32[4096]{0:T(1024)S(1)}, bf16[4096,128]{0,1:T(8,128)(2,1)}, /*index=5*/bf16[2,3,512,64]{2,3,1,0:T(8,128)(2,1)S(1)}, ...), branch_computations={%region_3.4_spmd, %region_4.9_spmd} | conditional | flops 848380416 | bytes 44134744 | solution.py:172
  136.9 99.9 %while.17 = (s32[]{:T(128)}, f32[2,3,512]{2,1,0:T(4,128)S(1)}, f32[2,3,512]{2,1,0:T(4,128)}, f32[2,3,512,64]{2,3,1,0:T(8,128)}, s32[512]{0:T(512)S(1)}, /*index=...) while((s32[]{:T(128)}, f32[2,3,512]{2,1,0:T(4,128)S(1)}, ...), condition=%wide.region_8.8_spmd.clone, body=%wide.region_5.7_spmd.clone.sunk | while | flops 848379904 | bytes 44130508 | solution.py:170
  136.9 0.8 compare_and_fusion.2
  137.8 1.0 constant_dynamic-slice_fusion.4
  138.7 6.7 %fusion.87 = (f32[2,3,512]{2,1,0:T(4,128)S(1)}, f32[2,1024,3,512]{3,1,2,0:T(8,128)}) fusion(pred[512,1024]{0,1:T(8,128)(4,1)S(1)} %compare_and_fusion.2, bf16[1024,2,64,1]{0,2,3,1:T(8,128)(2,1)S(1)} %bitcast.98, bf16[2,3,512,64]{2,3,1,0:T(8,128)(2,1)S(1)} %get-tuple-element.398), kind=kOutput, calls=%fused_computation.2.clone.1 | convolution fusion | flops 412087296 | bytes 13774848 | tf_op jit(solution)/shard_map/cond/branch_1_fun/while/body/eval_jaxpr/grqd,kgd->grqk/dot_general | solution.py:152
  145.4 6.5 %fusion.88 = f32[2,3,512]{2,1,0:T(4,128)S(1)} fusion(f32[2,1024,3,512]{3,1,2,0:T(8,128)} %get-tuple-element.359, f32[2,3,512]{2,1,0:T(4,128)S(1)} %select_maximum_fusion.2, pred[512,1024]{0,1:T(8,128)(4,1)S(1)} %compare_and_fusion.2), kind=kLoop, calls=%fused_computation.4.clone.1 | loop fusion | flops 15725568 | bytes 13131776 | tf_op jit(solution)/shard_map/cond/branch_1_fun/while/body/eval_jaxpr/reduce_sum | solution.py:161
  152.0 0.6 fusion.89
  152.6 1.0 constant_dynamic-slice_fusion.5
  153.7 7.4 %fusion.90 = f32[2,3,512,64]{2,3,1,0:T(8,128)} fusion(bf16[1024,2,64,1]{0,2,3,1:T(8,128)(2,1)S(1)} %bitcast.101, f32[2,1024,3,512]{3,1,2,0:T(8,128)} %get-tuple-element.359, f32[2,3,512]{2,1,0:T(4,128)S(1)} %select_maximum_fusion.2, pred[512,1024]{0,1:T(8,128)(4,1)S(1)} %compare_and_fusion.2, f32[2,3,512,64]{2,3,1,0:T(8,128)} %get-tuple-element.379, ...), kind=kOutput, calls=%fused_computation.8.clone.1 | convolution fusion | flops 418971648 | bytes 14966785 | tf_op jit(solution)/shard_map/cond/branch_1_fun/while/body/eval_jaxpr/grqk,kgd->grqd/dot_general | solution.py:162
  161.2 0.8 compare_and_fusion.2
  162.0 1.0 constant_dynamic-slice_fusion.4
  163.0 6.7 %fusion.87 = (f32[2,3,512]{2,1,0:T(4,128)S(1)}, f32[2,1024,3,512]{3,1,2,0:T(8,128)}) fusion(pred[512,1024]{0,1:T(8,128)(4,1)S(1)} %compare_and_fusion.2, bf16[1024,2,64,1]{0,2,3,1:T(8,128)(2,1)S(1)} %bitcast.98, bf16[2,3,512,64]{2,3,1,0:T(8,128)(2,1)S(1)} %get-tuple-element.398), kind=kOutput, calls=%fused_computation.2.clone.1 | convolution fusion | flops 412087296 | bytes 13774848 | tf_op jit(solution)/shard_map/cond/branch_1_fun/while/body/eval_jaxpr/grqd,kgd->grqk/dot_general | solution.py:152
  169.7 6.5 %fusion.88 = f32[2,3,512]{2,1,0:T(4,128)S(1)} fusion(f32[2,1024,3,512]{3,1,2,0:T(8,128)} %get-tuple-element.359, f32[2,3,512]{2,1,0:T(4,128)S(1)} %select_maximum_fusion.2, pred[512,1024]{0,1:T(8,128)(4,1)S(1)} %compare_and_fusion.2), kind=kLoop, calls=%fused_computation.4.clone.1 | loop fusion | flops 15725568 | bytes 13131776 | tf_op jit(solution)/shard_map/cond/branch_1_fun/while/body/eval_jaxpr/reduce_sum | solution.py:161
  176.2 1.4 fusion.89
  177.6 1.0 constant_dynamic-slice_fusion.5
  178.7 7.6 %fusion.90 = f32[2,3,512,64]{2,3,1,0:T(8,128)} fusion(bf16[1024,2,64,1]{0,2,3,1:T(8,128)(2,1)S(1)} %bitcast.101, f32[2,1024,3,512]{3,1,2,0:T(8,128)} %get-tuple-element.359, f32[2,3,512]{2,1,0:T(4,128)S(1)} %select_maximum_fusion.2, pred[512,1024]{0,1:T(8,128)(4,1)S(1)} %compare_and_fusion.2, f32[2,3,512,64]{2,3,1,0:T(8,128)} %get-tuple-element.379, ...), kind=kOutput, calls=%fused_computation.8.clone.1 | convolution fusion | flops 418971648 | bytes 14966785 | tf_op jit(solution)/shard_map/cond/branch_1_fun/while/body/eval_jaxpr/grqk,kgd->grqd/dot_general | solution.py:162
  186.4 0.8 compare_and_fusion.2
  187.2 1.0 constant_dynamic-slice_fusion.4
  188.2 6.7 %fusion.87 = (f32[2,3,512]{2,1,0:T(4,128)S(1)}, f32[2,1024,3,512]{3,1,2,0:T(8,128)}) fusion(pred[512,1024]{0,1:T(8,128)(4,1)S(1)} %compare_and_fusion.2, bf16[1024,2,64,1]{0,2,3,1:T(8,128)(2,1)S(1)} %bitcast.98, bf16[2,3,512,64]{2,3,1,0:T(8,128)(2,1)S(1)} %get-tuple-element.398), kind=kOutput, calls=%fused_computation.2.clone.1 | convolution fusion | flops 412087296 | bytes 13774848 | tf_op jit(solution)/shard_map/cond/branch_1_fun/while/body/eval_jaxpr/grqd,kgd->grqk/dot_general | solution.py:152
  194.9 6.5 %fusion.88 = f32[2,3,512]{2,1,0:T(4,128)S(1)} fusion(f32[2,1024,3,512]{3,1,2,0:T(8,128)} %get-tuple-element.359, f32[2,3,512]{2,1,0:T(4,128)S(1)} %select_maximum_fusion.2, pred[512,1024]{0,1:T(8,128)(4,1)S(1)} %compare_and_fusion.2), kind=kLoop, calls=%fused_computation.4.clone.1 | loop fusion | flops 15725568 | bytes 13131776 | tf_op jit(solution)/shard_map/cond/branch_1_fun/while/body/eval_jaxpr/reduce_sum | solution.py:161
  201.4 1.4 fusion.89
  202.8 1.0 constant_dynamic-slice_fusion.5
  203.9 7.6 %fusion.90 = f32[2,3,512,64]{2,3,1,0:T(8,128)} fusion(bf16[1024,2,64,1]{0,2,3,1:T(8,128)(2,1)S(1)} %bitcast.101, f32[2,1024,3,512]{3,1,2,0:T(8,128)} %get-tuple-element.359, f32[2,3,512]{2,1,0:T(4,128)S(1)} %select_maximum_fusion.2, pred[512,1024]{0,1:T(8,128)(4,1)S(1)} %compare_and_fusion.2, f32[2,3,512,64]{2,3,1,0:T(8,128)} %get-tuple-element.379, ...), kind=kOutput, calls=%fused_computation.8.clone.1 | convolution fusion | flops 418971648 | bytes 14966785 | tf_op jit(solution)/shard_map/cond/branch_1_fun/while/body/eval_jaxpr/grqk,kgd->grqd/dot_general | solution.py:162
  211.5 0.8 compare_and_fusion.2
  212.4 1.0 constant_dynamic-slice_fusion.4
  213.4 6.7 %fusion.87 = (f32[2,3,512]{2,1,0:T(4,128)S(1)}, f32[2,1024,3,512]{3,1,2,0:T(8,128)}) fusion(pred[512,1024]{0,1:T(8,128)(4,1)S(1)} %compare_and_fusion.2, bf16[1024,2,64,1]{0,2,3,1:T(8,128)(2,1)S(1)} %bitcast.98, bf16[2,3,512,64]{2,3,1,0:T(8,128)(2,1)S(1)} %get-tuple-element.398), kind=kOutput, calls=%fused_computation.2.clone.1 | convolution fusion | flops 412087296 | bytes 13774848 | tf_op jit(solution)/shard_map/cond/branch_1_fun/while/body/eval_jaxpr/grqd,kgd->grqk/dot_general | solution.py:152
  220.1 6.5 %fusion.88 = f32[2,3,512]{2,1,0:T(4,128)S(1)} fusion(f32[2,1024,3,512]{3,1,2,0:T(8,128)} %get-tuple-element.359, f32[2,3,512]{2,1,0:T(4,128)S(1)} %select_maximum_fusion.2, pred[512,1024]{0,1:T(8,128)(4,1)S(1)} %compare_and_fusion.2), kind=kLoop, calls=%fused_computation.4.clone.1 | loop fusion | flops 15725568 | bytes 13131776 | tf_op jit(solution)/shard_map/cond/branch_1_fun/while/body/eval_jaxpr/reduce_sum | solution.py:161
  226.6 1.4 fusion.89
  228.0 1.0 constant_dynamic-slice_fusion.5
  229.1 7.6 %fusion.90 = f32[2,3,512,64]{2,3,1,0:T(8,128)} fusion(bf16[1024,2,64,1]{0,2,3,1:T(8,128)(2,1)S(1)} %bitcast.101, f32[2,1024,3,512]{3,1,2,0:T(8,128)} %get-tuple-element.359, f32[2,3,512]{2,1,0:T(4,128)S(1)} %select_maximum_fusion.2, pred[512,1024]{0,1:T(8,128)(4,1)S(1)} %compare_and_fusion.2, f32[2,3,512,64]{2,3,1,0:T(8,128)} %get-tuple-element.379, ...), kind=kOutput, calls=%fused_computation.8.clone.1 | convolution fusion | flops 418971648 | bytes 14966785 | tf_op jit(solution)/shard_map/cond/branch_1_fun/while/body/eval_jaxpr/grqk,kgd->grqd/dot_general | solution.py:162
  236.8 1.3 divide_convert_fusion
  238.1 2.2 convolution_convert_fusion.1
  240.3 27.0 %reduce-scatter.3.cloned.1.call-done = bf16[128,1536]{1,0:T(8,128)(2,1)} async-done(((bf16[512,1536]{1,0:T(8,128)(2,1)}), bf16[128,1536]{1,0:T(8,128)(2,1)}) %reduce-scatter.3.cloned.1.call-update) | async-done | bytes 393232 | tf_op jit(solution)/shard_map/reduce_scatter | solution.py:179
  267.3 1.2 multiply_reduce_fusion
  268.6 1.9 multiply_convert_fusion
  270.6 5.5 %all_gather.22 = f32[512,40]{0,1:T(8,128)S(1)} all-gather(f32[128,40]{0,1:T(8,128)S(1)} %select_reduce_fusion.1), channel_id=1, replica_groups=mesh['req'=8,'ep'=4] {'ep'}, dimensions={0}, use_global_device_ids=true | all-gather | bytes 102400 | tf_op jit(solution)/shard_map/all_gather | solution.py:197
  276.9 0.9 select_reduce_fusion
  277.8 12.5 %all-gather.12.cloned.1.call-done = bf16[512,1536]{1,0:T(8,128)(2,1)} async-done(((bf16[128,1536]{1,0:T(8,128)(2,1)}), bf16[512,1536]{1,0:T(8,128)(2,1)}) %all-gather.12.cloned.1.call-update) | async-done | bytes 1572880 | tf_op jit(solution)/shard_map/all_gather | solution.py:196
  290.4 17.3 %fusion.19 = f32[10,192,1024]{2,1,0:T(8,128)} fusion(bf16[10,1536,1024]{2,1,0:T(8,128)(2,1)} %param.28, s32[10,512]{1,0:T(8,128)S(1)} %copy.55, pred[10,512]{1,0:T(8,128)(4,1)S(1)} %get-tuple-element.283, bf16[512,1536]{1,0:T(8,128)(2,1)} %all-gather.12.cloned.1.call-done), kind=kOutput, calls=%fused_computation.28 | convolution fusion | flops 9064611840 | bytes 40920064 | tf_op jit(solution)/shard_map/esd,edf->esf/dot_general | solution.py:211
  307.6 13.6 %fusion.40 = bf16[10,192,1536]{2,1,0:T(8,128)(2,1)} fusion(bf16[10,512,1536]{2,1,0:T(8,128)(2,1)} %param.29, f32[10,192,1024]{2,1,0:T(8,128)} %fusion.19), kind=kOutput, calls=%fused_computation.41 | convolution fusion | flops 3025797120 | bytes 29491200 | tf_op jit(solution)/shard_map/esf,efd->esd/dot_general | solution.py:215
  321.2 15.9 %fusion.35 = bf16[512,1536]{1,0:T(8,128)(2,1)} fusion(f32[10,192]{1,0:T(8,128)S(1)} %select_reduce_fusion, bf16[10,192,1536]{2,1,0:T(8,128)(2,1)} %fusion.40, s32[10,512]{1,0:T(8,128)S(1)} %copy.55, pred[10,512]{1,0:T(8,128)(4,1)S(1)} %get-tuple-element.283), kind=kOutput, calls=%fused_computation.38 | convolution fusion | flops 18128044032 | bytes 7504384 | tf_op jit(solution)/shard_map/esr,esd->rd/dot_general | solution.py:220
  337.2 1.5 reshape.181
  338.9 2.3 reshape.178
  341.2 3.0 copy.56
  344.2 0.8 reshape.179
  345.0 0.6 copy.64
  345.6 1.1 copy-done.2
  346.7 2.7 pad_maximum_fusion
  349.4 5.0 %reshape.180 = bf16[64,16384]{1,0:T(8,128)(2,1)S(1)} reshape(bf16[64,2,2,64,64]{4,3,2,1,0:T(8,128)(2,1)} %pad_maximum_fusion) | data formatting | bytes 4194304 | tf_op jit(solution)/shard_map/reshape | solution.py:123
  354.4 2.3 fusion.13
  356.7 2.7 reshape.182
  359.4 6.1 %reduce-scatter.5.cloned.1.call-done = bf16[128,1536]{1,0:T(8,128)(2,1)} async-done(((bf16[512,1536]{1,0:T(8,128)(2,1)}), bf16[128,1536]{1,0:T(8,128)(2,1)}) %reduce-scatter.5.cloned.1.call-update) | async-done | bytes 393232 | tf_op jit(solution)/shard_map/reduce_scatter | solution.py:227
  (90 shorter events, 3.5 us)
Async XLA Ops:
  7.2 230.9 %copy-start = (bf16[384,1536]{1,0:T(8,128)(2,1)S(1)}, bf16[384,1536]{1,0:T(8,128)(2,1)}, u32[]{:S(2)}) copy-start(bf16[384,1536]{1,0:T(8,128)(2,1)} %param.27) | copy-start | bytes 3538948
  7.2 47.6 %all-gather.6.cloned.1.call-start = ((), (), s32[]{:S(2)}) async-start(), calls=%async_computation.2 | async-start | bytes 1966080 | tf_op jit(solution)/shard_map/all_gather | solution.py:76
  10.4 84.7 %all-gather.8.cloned.1.call-start = ((), (), s32[]{:S(2)}) async-start(), calls=%async_computation.3 | async-start | bytes 1179648 | tf_op jit(solution)/shard_map/all_gather | solution.py:113
  58.2 4.4 %copy-start.6 = (f32[512,640]{1,0:T(8,128)}, f32[512,640]{1,0:T(8,128)S(1)}, u32[]{:S(2)}) copy-start(f32[512,640]{1,0:T(8,128)S(1)} %fusion.42) | copy-start | bytes 3932164
  59.3 77.5 %all-gather.10.cloned.1.call-start = ((), (), s32[]{:S(2)}) async-start(), calls=%async_computation.4 | async-start | bytes 1179648 | tf_op jit(solution)/shard_map/all_gather | solution.py:114
  60.1 207.3 %reduce-scatter.3.cloned.1.call-start = ((), (), s32[]{:S(2)}) async-start(), calls=%async_computation.5 | async-start | bytes 1966080 | tf_op jit(solution)/shard_map/reduce_scatter | solution.py:179
  236.7 30.6 %copy-start.3 = (bf16[128,1536]{1,0:T(8,128)(2,1)S(1)}, bf16[128,1536]{1,0:T(8,128)(2,1)}, u32[]{:S(2)}) copy-start(bf16[128,1536]{1,0:T(8,128)(2,1)} %param.18) | copy-start | bytes 1179652
  236.7 31.8 %copy-start.8 = (f32[1536]{0:T(1024)S(1)}, f32[1536]{0:T(1024)}, u32[]{:S(2)}) copy-start(f32[1536]{0:T(1024)} %param.23) | copy-start | bytes 18436
  236.7 33.8 %copy-start.9 = (f32[128,8]{0,1:T(8,128)S(1)}, f32[128,8]{0,1:T(8,128)}, u32[]{:S(2)}) copy-start(f32[128,8]{0,1:T(8,128)} %param.21) | copy-start | bytes 12292
  236.8 33.8 %copy-start.10 = (s32[128,8]{0,1:T(8,128)S(1)}, s32[128,8]{0,1:T(8,128)}, u32[]{:S(2)}) copy-start(s32[128,8]{0,1:T(8,128)} %param.20) | copy-start | bytes 12292
  240.3 50.1 %all-gather.12.cloned.1.call-start = ((), (), s32[]{:S(2)}) async-start(), calls=%async_computation.6 | async-start | bytes 1966080 | tf_op jit(solution)/shard_map/all_gather | solution.py:196
  270.5 95.0 %reduce-scatter.5.cloned.1.call-start = ((), (), s32[]{:S(2)}) async-start(), calls=%async_computation.7 | async-start | bytes 1966080 | tf_op jit(solution)/shard_map/reduce_scatter | solution.py:227
  321.2 16.0 %copy-start.7 = (bf16[12,2,2,64,64]{4,3,2,1,0:T(8,128)(2,1)S(1)}, bf16[12,2,2,64,64]{4,3,2,1,0:T(8,128)(2,1)}, u32[]{:S(2)}) copy-start(bf16[12,2,2,64,64]{4,3,2,1,0:T(8,128)(2,1)} %param.30) | copy-start | bytes 1179652
  321.2 17.5 %copy-start.11 = (s32[64]{0:T(128)S(1)}, s32[64]{0:T(128)}, u32[]{:S(2)}) copy-start(s32[64]{0:T(128)} %param.31) | copy-start | bytes 772
  321.2 17.7 %copy-start.4 = (bf16[4096,128]{0,1:T(8,128)(2,1)S(1)}, bf16[4096,128]{0,1:T(8,128)(2,1)}, u32[]{:S(2)}) copy-start(bf16[4096,128]{0,1:T(8,128)(2,1)} %all-gather.8.cloned.1.call-done) | copy-start | bytes 3145732
  341.2 3.0 copy-start.5
  345.0 1.7 copy-start.2
  346.7 18.9 %copy-start.1 = (bf16[384,1536]{1,0:T(8,128)(2,1)S(1)}, bf16[384,1536]{1,0:T(8,128)(2,1)}, u32[]{:S(2)}) copy-start(bf16[384,1536]{1,0:T(8,128)(2,1)} %param.27) | copy-start | bytes 3538948
Sparse Core Ops, SparseCore 0:
  10.5 22.3 all-gather.5
  59.4 35.5 all-gather.7
  97.8 39.0 all-gather.9
  240.4 26.9 reduce-scatter.2
  270.7 19.6 all-gather.11
  337.3 28.1 reduce-scatter.4
where the time goes:
time: 373 us; the launch traced here: 372 us
  waiting for transfers between devices  118 us (32%)
  matrix products  112 us (30%)
  blocking collectives  48.7 us (13%)
  other arithmetic  48.2 us (13%)
  local copies, waits for them, and re-layouts  29.4 us (8%)
  between operations  15.7 us (4%)
    all_gather x1, blocking collectives, body(): all_segs = lax.all_gather(seg_ids, ('req', 'ep'), axis=0, tiled=True)  43.2 us
    all_gather x1, waiting for transfers between devices, body(): value_piece = lax.all_gather(value_rows, 'req', axis=0, tiled=True)  41.8 us
    all_gather x1, waiting for transfers between devices, body(): key_piece = lax.all_gather(key_matrix, 'req', axis=0, tiled=True)  30.8 us
    dot_general x4, matrix products, one_block(): jnp.einsum('grqk,kgd->grqd', exponent.astype(jnp.bfloat16), value_block,...  30.3 us
    reduce_scatter x1, waiting for transfers between devices, body(): lax.psum_scatter(jnp.dot(head_out, w_out_attn, preferred_element_type=jnp...  27 us
    dot_general x4, matrix products, one_block(): jnp.einsum('grqd,kgd->grqk', query_grouped, key_block, preferred_element_...  26.7 us
    reduce_sum x4, other arithmetic, one_block(): new_sum = block_sum * rescale + jnp.sum(exponent, axis=-1)  26.2 us
    dot_general x1, matrix products, body(): jnp.einsum('esd,edf->esf', arrived, w_in, preferred_element_type=jnp.floa...  17.3 us
  transfers between devices with their start and end apart: 6, of which 5 were waited for; matrix products, arithmetic and copies ran while one was open for 7% of the time, Pallas kernels for 0%

commit v1 on v0

--- a/solution.py
+++ b/solution.py
@@ -110,8 +110,13 @@
     run_sum = jnp.zeros((kv_heads, heads_ratio, group_len), jnp.float32)
     run_acc = jnp.zeros((kv_heads, heads_ratio, group_len, HEAD_SIZE), jnp.float32)
     cache_rows = paged_key_value_cache.reshape(pages_here, page_cells)
-    key_piece = lax.all_gather(key_matrix, "req", axis=0, tiled=True)
-    value_piece = lax.all_gather(value_rows, "req", axis=0, tiled=True)
+    key_piece, value_piece = jnp.split(
+        lax.all_gather(
+            jnp.concatenate([key_matrix, value_rows], axis=1), "req", axis=0, tiled=True
+        ),
+        [key_matrix.shape[1]],
+        axis=1,
+    )
     n_rows = key_piece.shape[0]
     piece_pages = n_rows // PAGE_TOKENS
     keys_paged = key_piece.reshape(piece_pages, PAGE_TOKENS, kv_heads, HEAD_SIZE).transpose(

time: 373 us -> 341 us (0.914)
  waiting for transfers between devices: 118 us -> 84.2 us
    all_gather x2 -> x1, waiting for transfers between devices: 72.6 us -> 41.5 us  [body(): lax.all_gather(jnp.concatenate([key_matrix, value_rows], axis=1), 'req',...]
  transfers between devices with their start and end apart: 6 -> 5, of which waited for: 5 -> 4; matrix products, arithmetic and copies ran while one was open for 7% -> 9% of each run, Pallas kernels for 0% -> 0%
where the time goes in v1:
time: 341 us; the launch traced here: 340 us
  matrix products  111 us (33%)
  waiting for transfers between devices  84.2 us (25%)
  blocking collectives  48.7 us (14%)
  other arithmetic  47.9 us (14%)
  local copies, waits for them, and re-layouts  32.9 us (10%)
  between operations  15.3 us (4%)
    all_gather x1, blocking collectives, body(): all_segs = lax.all_gather(seg_ids, ('req', 'ep'), axis=0, tiled=True)  43.2 us
    all_gather x1, waiting for transfers between devices, body(): lax.all_gather(jnp.concatenate([key_matrix, value_rows], axis=1), 'req',...  41.5 us
    dot_general x4, matrix products, one_block(): jnp.einsum('grqk,kgd->grqd', exponent.astype(jnp.bfloat16), value_block,...  30.3 us
    reduce_scatter x1, waiting for transfers between devices, body(): lax.psum_scatter(jnp.dot(head_out, w_out_attn, preferred_element_type=jnp...  26.8 us
    dot_general x4, matrix products, one_block(): jnp.einsum('grqd,kgd->grqk', query_grouped, key_block, preferred_element_...  26.7 us
    reduce_sum x4, other arithmetic, one_block(): new_sum = block_sum * rescale + jnp.sum(exponent, axis=-1)  26.2 us
    dot_general x1, matrix products, body(): jnp.einsum('esd,edf->esf', arrived, w_in, preferred_element_type=jnp.floa...  17.3 us
    dot_general x1, matrix products, body(): jnp.einsum('esr,esd->rd', dispatch.astype(jnp.float32), weighted, precisi...  15.5 us
  transfers between devices with their start and end apart: 5, of which 4 were waited for; matrix products, arithmetic and copies ran while one was open for 9% of the time, Pallas kernels for 0%

profile of v1, /device:TPU:0, one launch (start us, length us, event | category | flops | bytes accessed | tf_op | source)
XLA Modules:
  0.0 340.5 jit_solution(5574905531903767057)
XLA Ops:
  7.2 1.2 fusion.57
  8.5 1.9 fusion.59
  10.5 43.2 %all-gather = s32[32,1,128]{2,1,0:T(1,128)S(1)} all-gather(s32[1,1,128]{2,1,0:T(1,128)} %bitcast.111), channel_id=1, replica_groups=mesh['req'=8,'ep'=4] {'req','ep'}, dimensions={0}, use_global_device_ids=true | all-gather | bytes 16896 | tf_op jit(solution)/shard_map/all_gather | solution.py:68
  53.8 0.3 reduce-window.9
  54.5 0.3 multiply_cosine_fusion
  54.8 3.4 fusion.42
  58.2 1.0 copy-done.3
  59.6 0.7 pad_maximum_fusion.1
  60.4 0.6 dynamic_slice.41
  61.1 0.5 slice.42
  62.8 1.2 slice.62
  64.0 0.3 copy.56
  64.5 41.5 %all-gather.7.cloned.1.call-done = bf16[4096,256]{1,0:T(8,128)(2,1)} async-done(((bf16[512,256]{1,0:T(8,128)(2,1)}), bf16[4096,256]{1,0:T(8,128)(2,1)}) %all-gather.7.cloned.1.call-update) | async-done | bytes 2097168 | tf_op jit(solution)/shard_map/all_gather | solution.py:114
  105.9 3.0 fusion.66
  108.9 96.9 %conditional.1 = (f32[2,3,512]{2,1,0:T(4,128)}, f32[2,3,512,64]{2,3,1,0:T(8,128)}) conditional(s32[]{:T(128)} %convert_element_type.66, () %tuple.30, (s32[]{:T(128)}, s32[512]{0:T(512)S(1)}, s32[512]{0:T(512)S(1)}, s32[4096]{0:T(1024)S(1)}, bf16[4096,128]{1,0:T(8,128)(2,1)}, /*index=5*/bf16[2,3,512,64]{2,3,1,0:T(8,128)(2,1)S(1)}, ...), branch_computations={%region_3.4_spmd, %region_4.9_spmd} | conditional | flops 848380416 | bytes 44659036 | solution.py:177
  108.9 96.9 %while.17 = (s32[]{:T(128)}, f32[2,3,512]{2,1,0:T(4,128)S(1)}, f32[2,3,512]{2,1,0:T(4,128)}, f32[2,3,512,64]{2,3,1,0:T(8,128)}, s32[512]{0:T(512)S(1)}, /*index=...) while((s32[]{:T(128)}, f32[2,3,512]{2,1,0:T(4,128)S(1)}, ...), condition=%wide.region_8.8_spmd.clone, body=%wide.region_5.7_spmd.clone.sunk | while | flops 848379904 | bytes 44654800 | solution.py:175
  109.0 0.8 compare_and_fusion.2
  109.8 1.1 constant_dynamic-slice_fusion.3
  110.9 0.1 copy.73
  111.0 6.7 %fusion.88 = (f32[2,3,512]{2,1,0:T(4,128)S(1)}, f32[2,1024,3,512]{3,1,2,0:T(8,128)}) fusion(pred[512,1024]{0,1:T(8,128)(4,1)S(1)} %compare_and_fusion.2, bf16[1024,2,64,1]{0,2,3,1:T(8,128)(2,1)S(1)} %bitcast.96, bf16[2,3,512,64]{2,3,1,0:T(8,128)(2,1)S(1)} %get-tuple-element.408), kind=kOutput, calls=%fused_computation.2.clone.1 | convolution fusion | flops 412087296 | bytes 13774848 | tf_op jit(solution)/shard_map/cond/branch_1_fun/while/body/eval_jaxpr/grqd,kgd->grqk/dot_general | solution.py:157
  117.7 6.5 %fusion.89 = f32[2,3,512]{2,1,0:T(4,128)S(1)} fusion(f32[2,1024,3,512]{3,1,2,0:T(8,128)} %get-tuple-element.368, f32[2,3,512]{2,1,0:T(4,128)S(1)} %select_maximum_fusion.2, pred[512,1024]{0,1:T(8,128)(4,1)S(1)} %compare_and_fusion.2), kind=kLoop, calls=%fused_computation.4.clone.1 | loop fusion | flops 15725568 | bytes 13131776 | tf_op jit(solution)/shard_map/cond/branch_1_fun/while/body/eval_jaxpr/reduce_sum | solution.py:166
  124.3 0.6 fusion.90
  125.1 7.4 %fusion.91 = f32[2,3,512,64]{2,3,1,0:T(8,128)} fusion(bf16[1024,2,64,1]{0,2,3,1:T(8,128)(2,1)S(1)} %bitcast.97, f32[2,1024,3,512]{3,1,2,0:T(8,128)} %get-tuple-element.368, f32[2,3,512]{2,1,0:T(4,128)S(1)} %select_maximum_fusion.2, pred[512,1024]{0,1:T(8,128)(4,1)S(1)} %compare_and_fusion.2, f32[2,3,512,64]{2,3,1,0:T(8,128)} %get-tuple-element.389, ...), kind=kOutput, calls=%fused_computation.8.clone.1 | convolution fusion | flops 418971648 | bytes 14966785 | tf_op jit(solution)/shard_map/cond/branch_1_fun/while/body/eval_jaxpr/grqk,kgd->grqd/dot_general | solution.py:167
  132.5 0.8 compare_and_fusion.2
  133.3 1.1 constant_dynamic-slice_fusion.3
  134.4 0.1 copy.73
  134.5 6.7 %fusion.88 = (f32[2,3,512]{2,1,0:T(4,128)S(1)}, f32[2,1024,3,512]{3,1,2,0:T(8,128)}) fusion(pred[512,1024]{0,1:T(8,128)(4,1)S(1)} %compare_and_fusion.2, bf16[1024,2,64,1]{0,2,3,1:T(8,128)(2,1)S(1)} %bitcast.96, bf16[2,3,512,64]{2,3,1,0:T(8,128)(2,1)S(1)} %get-tuple-element.408), kind=kOutput, calls=%fused_computation.2.clone.1 | convolution fusion | flops 412087296 | bytes 13774848 | tf_op jit(solution)/shard_map/cond/branch_1_fun/while/body/eval_jaxpr/grqd,kgd->grqk/dot_general | solution.py:157
  141.2 6.5 %fusion.89 = f32[2,3,512]{2,1,0:T(4,128)S(1)} fusion(f32[2,1024,3,512]{3,1,2,0:T(8,128)} %get-tuple-element.368, f32[2,3,512]{2,1,0:T(4,128)S(1)} %select_maximum_fusion.2, pred[512,1024]{0,1:T(8,128)(4,1)S(1)} %compare_and_fusion.2), kind=kLoop, calls=%fused_computation.4.clone.1 | loop fusion | flops 15725568 | bytes 13131776 | tf_op jit(solution)/shard_map/cond/branch_1_fun/while/body/eval_jaxpr/reduce_sum | solution.py:166
  147.8 1.4 fusion.90
  149.3 7.6 %fusion.91 = f32[2,3,512,64]{2,3,1,0:T(8,128)} fusion(bf16[1024,2,64,1]{0,2,3,1:T(8,128)(2,1)S(1)} %bitcast.97, f32[2,1024,3,512]{3,1,2,0:T(8,128)} %get-tuple-element.368, f32[2,3,512]{2,1,0:T(4,128)S(1)} %select_maximum_fusion.2, pred[512,1024]{0,1:T(8,128)(4,1)S(1)} %compare_and_fusion.2, f32[2,3,512,64]{2,3,1,0:T(8,128)} %get-tuple-element.389, ...), kind=kOutput, calls=%fused_computation.8.clone.1 | convolution fusion | flops 418971648 | bytes 14966785 | tf_op jit(solution)/shard_map/cond/branch_1_fun/while/body/eval_jaxpr/grqk,kgd->grqd/dot_general | solution.py:167
  156.9 0.8 compare_and_fusion.2
  157.8 1.1 constant_dynamic-slice_fusion.3
  159.0 6.7 %fusion.88 = (f32[2,3,512]{2,1,0:T(4,128)S(1)}, f32[2,1024,3,512]{3,1,2,0:T(8,128)}) fusion(pred[512,1024]{0,1:T(8,128)(4,1)S(1)} %compare_and_fusion.2, bf16[1024,2,64,1]{0,2,3,1:T(8,128)(2,1)S(1)} %bitcast.96, bf16[2,3,512,64]{2,3,1,0:T(8,128)(2,1)S(1)} %get-tuple-element.408), kind=kOutput, calls=%fused_computation.2.clone.1 | convolution fusion | flops 412087296 | bytes 13774848 | tf_op jit(solution)/shard_map/cond/branch_1_fun/while/body/eval_jaxpr/grqd,kgd->grqk/dot_general | solution.py:157
  165.7 6.5 %fusion.89 = f32[2,3,512]{2,1,0:T(4,128)S(1)} fusion(f32[2,1024,3,512]{3,1,2,0:T(8,128)} %get-tuple-element.368, f32[2,3,512]{2,1,0:T(4,128)S(1)} %select_maximum_fusion.2, pred[512,1024]{0,1:T(8,128)(4,1)S(1)} %compare_and_fusion.2), kind=kLoop, calls=%fused_computation.4.clone.1 | loop fusion | flops 15725568 | bytes 13131776 | tf_op jit(solution)/shard_map/cond/branch_1_fun/while/body/eval_jaxpr/reduce_sum | solution.py:166
  172.2 1.4 fusion.90
  173.7 7.6 %fusion.91 = f32[2,3,512,64]{2,3,1,0:T(8,128)} fusion(bf16[1024,2,64,1]{0,2,3,1:T(8,128)(2,1)S(1)} %bitcast.97, f32[2,1024,3,512]{3,1,2,0:T(8,128)} %get-tuple-element.368, f32[2,3,512]{2,1,0:T(4,128)S(1)} %select_maximum_fusion.2, pred[512,1024]{0,1:T(8,128)(4,1)S(1)} %compare_and_fusion.2, f32[2,3,512,64]{2,3,1,0:T(8,128)} %get-tuple-element.389, ...), kind=kOutput, calls=%fused_computation.8.clone.1 | convolution fusion | flops 418971648 | bytes 14966785 | tf_op jit(solution)/shard_map/cond/branch_1_fun/while/body/eval_jaxpr/grqk,kgd->grqd/dot_general | solution.py:167
  181.4 0.8 compare_and_fusion.2
  182.2 1.1 constant_dynamic-slice_fusion.3
  183.4 6.7 %fusion.88 = (f32[2,3,512]{2,1,0:T(4,128)S(1)}, f32[2,1024,3,512]{3,1,2,0:T(8,128)}) fusion(pred[512,1024]{0,1:T(8,128)(4,1)S(1)} %compare_and_fusion.2, bf16[1024,2,64,1]{0,2,3,1:T(8,128)(2,1)S(1)} %bitcast.96, bf16[2,3,512,64]{2,3,1,0:T(8,128)(2,1)S(1)} %get-tuple-element.408), kind=kOutput, calls=%fused_computation.2.clone.1 | convolution fusion | flops 412087296 | bytes 13774848 | tf_op jit(solution)/shard_map/cond/branch_1_fun/while/body/eval_jaxpr/grqd,kgd->grqk/dot_general | solution.py:157
  190.1 6.5 %fusion.89 = f32[2,3,512]{2,1,0:T(4,128)S(1)} fusion(f32[2,1024,3,512]{3,1,2,0:T(8,128)} %get-tuple-element.368, f32[2,3,512]{2,1,0:T(4,128)S(1)} %select_maximum_fusion.2, pred[512,1024]{0,1:T(8,128)(4,1)S(1)} %compare_and_fusion.2), kind=kLoop, calls=%fused_computation.4.clone.1 | loop fusion | flops 15725568 | bytes 13131776 | tf_op jit(solution)/shard_map/cond/branch_1_fun/while/body/eval_jaxpr/reduce_sum | solution.py:166
  196.7 1.4 fusion.90
  198.2 7.6 %fusion.91 = f32[2,3,512,64]{2,3,1,0:T(8,128)} fusion(bf16[1024,2,64,1]{0,2,3,1:T(8,128)(2,1)S(1)} %bitcast.97, f32[2,1024,3,512]{3,1,2,0:T(8,128)} %get-tuple-element.368, f32[2,3,512]{2,1,0:T(4,128)S(1)} %select_maximum_fusion.2, pred[512,1024]{0,1:T(8,128)(4,1)S(1)} %compare_and_fusion.2, f32[2,3,512,64]{2,3,1,0:T(8,128)} %get-tuple-element.389, ...), kind=kOutput, calls=%fused_computation.8.clone.1 | convolution fusion | flops 418971648 | bytes 14966785 | tf_op jit(solution)/shard_map/cond/branch_1_fun/while/body/eval_jaxpr/grqk,kgd->grqd/dot_general | solution.py:167
  205.8 1.3 divide_convert_fusion
  207.1 2.2 convolution_convert_fusion.1
  209.4 26.8 %reduce-scatter.3.cloned.1.call-done = bf16[128,1536]{1,0:T(8,128)(2,1)} async-done(((bf16[512,1536]{1,0:T(8,128)(2,1)}), bf16[128,1536]{1,0:T(8,128)(2,1)}) %reduce-scatter.3.cloned.1.call-update) | async-done | bytes 393232 | tf_op jit(solution)/shard_map/reduce_scatter | solution.py:184
  236.1 1.2 multiply_reduce_fusion
  237.4 1.9 multiply_convert_fusion
  239.4 5.5 %all_gather.18 = f32[512,40]{0,1:T(8,128)S(1)} all-gather(f32[128,40]{0,1:T(8,128)S(1)} %select_reduce_fusion.1), channel_id=1, replica_groups=mesh['req'=8,'ep'=4] {'ep'}, dimensions={0}, use_global_device_ids=true | all-gather | bytes 102400 | tf_op jit(solution)/shard_map/all_gather | solution.py:202
  245.1 0.3 reduce_window_sum.11
  245.7 0.9 select_reduce_fusion
  246.6 12.5 %all-gather.9.cloned.1.call-done = bf16[512,1536]{1,0:T(8,128)(2,1)} async-done(((bf16[128,1536]{1,0:T(8,128)(2,1)}), bf16[512,1536]{1,0:T(8,128)(2,1)}) %all-gather.9.cloned.1.call-update) | async-done | bytes 1572880 | tf_op jit(solution)/shard_map/all_gather | solution.py:201
  259.1 17.3 %fusion.19 = f32[10,192,1024]{2,1,0:T(8,128)} fusion(bf16[10,1536,1024]{2,1,0:T(8,128)(2,1)} %param.28, s32[10,512]{1,0:T(8,128)S(1)} %copy.60, pred[10,512]{1,0:T(8,128)(4,1)S(1)} %get-tuple-element.283, bf16[512,1536]{1,0:T(8,128)(2,1)} %all-gather.9.cloned.1.call-done), kind=kOutput, calls=%fused_computation.28 | convolution fusion | flops 9064611840 | bytes 40920064 | tf_op jit(solution)/shard_map/esd,edf->esf/dot_general | solution.py:216
  276.4 13.6 %fusion.40 = bf16[10,192,1536]{2,1,0:T(8,128)(2,1)} fusion(bf16[10,512,1536]{2,1,0:T(8,128)(2,1)} %param.29, f32[10,192,1024]{2,1,0:T(8,128)} %fusion.19), kind=kOutput, calls=%fused_computation.42 | convolution fusion | flops 3025797120 | bytes 29491200 | tf_op jit(solution)/shard_map/esf,efd->esd/dot_general | solution.py:220
  290.0 15.5 %fusion.35 = bf16[512,1536]{1,0:T(8,128)(2,1)} fusion(f32[10,192]{1,0:T(8,128)S(1)} %select_reduce_fusion, bf16[10,192,1536]{2,1,0:T(8,128)(2,1)} %fusion.40, s32[10,512]{1,0:T(8,128)S(1)} %copy.60, pred[10,512]{1,0:T(8,128)(4,1)S(1)} %get-tuple-element.283), kind=kOutput, calls=%fused_computation.38 | convolution fusion | flops 18128044032 | bytes 7504384 | tf_op jit(solution)/shard_map/esr,esd->rd/dot_general | solution.py:225
  305.6 1.9 reshape.181
  307.6 0.2 compare_reduce_fusion
  307.7 5.0 %reshape.179 = bf16[64,64,2,64]{3,2,1,0:T(2,128)(2,1)} reshape(bf16[4096,128]{1,0:T(8,128)(2,1)} %get-tuple-element.289) | data formatting | bytes 2097152 | tf_op jit(solution)/shard_map/reshape | solution.py:125
  312.8 1.8 reshape.178
  314.6 3.5 %copy_bitcast_fusion = (bf16[64,2,1,64,64]{4,3,2,1,0:T(8,128)(2,1)S(1)}, bf16[64,2,1,64,64]{4,3,2,1,0:T(8,128)(2,1)S(1)}) fusion(bf16[64,64,2,64]{3,2,1,0:T(2,128)(2,1)} %reshape.179, bf16[64,64,2,64]{3,2,1,0:T(2,128)(2,1)} %reshape.178), kind=kLoop, calls=%fused_computation.40 | loop fusion | bytes 4194304 | tf_op jit(solution)/shard_map/stack | solution.py:128
  318.1 2.7 pad_maximum_fusion
  320.8 6.0 %reshape.180 = bf16[64,16384]{1,0:T(8,128)(2,1)} reshape(bf16[64,2,2,64,64]{4,3,2,1,0:T(8,128)(2,1)} %pad_maximum_fusion) | data formatting | bytes 4194304 | tf_op jit(solution)/shard_map/reshape | solution.py:128
  326.8 2.1 fusion.13
  328.9 1.7 reshape.182
  330.6 3.3 reduce-scatter.5.cloned.1.call-done
  (81 shorter events, 2.9 us)
Async XLA Ops:
  7.2 199.9 %copy-start = (bf16[384,1536]{1,0:T(8,128)(2,1)S(1)}, bf16[384,1536]{1,0:T(8,128)(2,1)}, u32[]{:S(2)}) copy-start(bf16[384,1536]{1,0:T(8,128)(2,1)} %param.27) | copy-start | bytes 3538948
  7.2 47.6 %all-gather.5.cloned.1.call-start = ((), (), s32[]{:S(2)}) async-start(), calls=%async_computation.2 | async-start | bytes 1966080 | tf_op jit(solution)/shard_map/all_gather | solution.py:76
  10.4 95.5 %all-gather.7.cloned.1.call-start = ((), (), s32[]{:S(2)}) async-start(), calls=%async_computation.3 | async-start | bytes 2359296 | tf_op jit(solution)/shard_map/all_gather | solution.py:114
  58.2 1.1 copy-start.3
  60.4 175.8 %reduce-scatter.3.cloned.1.call-start = ((), (), s32[]{:S(2)}) async-start(), calls=%async_computation.4 | async-start | bytes 1966080 | tf_op jit(solution)/shard_map/reduce_scatter | solution.py:184
  205.8 30.3 %copy-start.2 = (bf16[128,1536]{1,0:T(8,128)(2,1)S(1)}, bf16[128,1536]{1,0:T(8,128)(2,1)}, u32[]{:S(2)}) copy-start(bf16[128,1536]{1,0:T(8,128)(2,1)} %param.18) | copy-start | bytes 1179652
  205.8 31.6 %copy-start.4 = (f32[1536]{0:T(1024)S(1)}, f32[1536]{0:T(1024)}, u32[]{:S(2)}) copy-start(f32[1536]{0:T(1024)} %param.23) | copy-start | bytes 18436
  205.8 33.6 %copy-start.5 = (f32[128,8]{0,1:T(8,128)S(1)}, f32[128,8]{0,1:T(8,128)}, u32[]{:S(2)}) copy-start(f32[128,8]{0,1:T(8,128)} %param.21) | copy-start | bytes 12292
  205.8 33.6 %copy-start.6 = (s32[128,8]{0,1:T(8,128)S(1)}, s32[128,8]{0,1:T(8,128)}, u32[]{:S(2)}) copy-start(s32[128,8]{0,1:T(8,128)} %param.20) | copy-start | bytes 12292
  209.3 49.8 %all-gather.9.cloned.1.call-start = ((), (), s32[]{:S(2)}) async-start(), calls=%async_computation.5 | async-start | bytes 1966080 | tf_op jit(solution)/shard_map/all_gather | solution.py:201
  239.3 94.6 %reduce-scatter.5.cloned.1.call-start = ((), (), s32[]{:S(2)}) async-start(), calls=%async_computation.6 | async-start | bytes 1966080 | tf_op jit(solution)/shard_map/reduce_scatter | solution.py:232
  290.0 17.5 %copy-start.7 = (s32[64]{0:T(128)S(1)}, s32[64]{0:T(128)}, u32[]{:S(2)}) copy-start(s32[64]{0:T(128)} %param.31) | copy-start | bytes 772
  305.6 7.2 %copy-start.1 = (bf16[4096,128]{1,0:T(8,128)(2,1)S(1)}, bf16[4096,128]{1,0:T(8,128)(2,1)}, u32[]{:S(2)}) copy-start(bf16[4096,128]{1,0:T(8,128)(2,1)} %get-tuple-element.290) | copy-start | bytes 3145732
Sparse Core Ops, SparseCore 0:
  10.5 22.3 all-gather.4
  60.5 45.3 all-gather.6
  209.4 26.6 reduce-scatter.2
  239.4 19.6 all-gather.8
  305.7 28.1 reduce-scatter.4
